TPU v7x, 32 devices: a whole 2x2x4 slice. The times are simulated.
32 devices in a mesh: tok: 4 (over y, x), ka: 4 (over z), out: 2 (over core).
Axes of the slice: x: 2, y: 2, z: 4, core: 2. Of those that a mesh axis runs over, the one named last changes fastest.
Arguments:
- features: bfloat16 [1024, 12288], P('tok', ('ka', 'out')), may hold values from -12 to 12, as said below
- lengths: int32 [4], P('tok'), may hold values from 1 to 256, 768 in all
- w_qkv: bfloat16 [12288, 24576], P(('ka', 'tok'), 'out'), may hold values from -0.0546875 to 0.0546875
- b_qkv: bfloat16 [24576], P(('out', 'ka')), may hold values from -2 to 2
- w_out: bfloat16 [8192, 12288], P(('out', 'tok'), 'ka'), may hold values from -0.0625 to 0.0625
- b_out: bfloat16 [12288], P(('ka', 'out')), may hold values from -3 to 3
Outputs:
- result: float32 [1024, 12288], P('tok', ('ka', 'out'))
Inputs may be any that keep to these rules, and one draw needn't show every extreme that they name: features: activations of order one; rows may differ in scale. `lengths`: live tokens of each prompt; some prompt is full.
All inputs are finite; a program needn't handle non-finite values. No bound on the sum of `lengths` on one device may be relied on, other than what follows from the above.
Results may differ from a plain program's by a relative error of at most 0.008.
Values may be sent and summed in bfloat16 or wider, within the bound.
No kernel may reach another device: no remote copies, remote signals or barrier semaphores. Data moves between devices by JAX's collectives and lax.ppermute only.
A program may use at most 192 MiB of HBM per device.

v0:
```python
import jax
import jax.numpy as jnp
from jax import lax
from jax.sharding import PartitionSpec as P

HD = 128
SEQ = 256


def softmax_rows(scores, allowed):
    scores = jnp.where(allowed, scores, -1e30)
    row_max = jnp.max(scores, axis=-1, keepdims=True)
    weights = jnp.exp(scores - row_max)
    row_sum = jnp.sum(weights, axis=-1, keepdims=True)
    return (weights / row_sum).astype(jnp.bfloat16)


def shards(features, lengths, w_qkv, b_qkv, w_out, b_out):
    row_count = features.shape[0]
    prompts = row_count // SEQ
    score_scale = 1.0 / HD**0.5
    panel = lax.all_gather(features, "out", axis=1, tiled=True)
    w_block = lax.all_gather(w_qkv, "tok", axis=0, tiled=True)
    partial_value = jnp.dot(panel, w_block, preferred_element_type=jnp.float32)
    qkv_sum = lax.psum_scatter(
        partial_value.astype(jnp.bfloat16), "ka", scatter_dimension=1, tiled=True
    ).astype(jnp.float32)
    qkv_held = (qkv_sum + b_qkv.astype(jnp.float32)).astype(jnp.bfloat16)
    heads_dev = qkv_held.shape[1] // (3 * HD)
    table = qkv_held.reshape(prompts, SEQ, heads_dev, 3, HD)
    positions = jnp.arange(SEQ)
    causal = positions[None, :] <= positions[:, None]
    live = positions[None, :] < lengths[:, None]
    allowed = causal[None, None] & live[:, None, None, :]
    scores = (
        jnp.einsum(
            "pshd,pthd->phst",
            table[:, :, :, 0],
            table[:, :, :, 1],
            preferred_element_type=jnp.float32,
        )
        * score_scale
    )
    prob_rows = softmax_rows(scores, allowed)
    context = jnp.einsum(
        "phst,pthd->pshd", prob_rows, table[:, :, :, 2], preferred_element_type=jnp.float32
    )
    context = context.astype(jnp.bfloat16).reshape(row_count, heads_dev * HD)
    head_group = lax.all_gather(context, "ka", axis=1, tiled=True)
    terms = jnp.dot(
        head_group,
        lax.all_gather(w_out, "tok", axis=0, tiled=True),
        preferred_element_type=jnp.float32,
    )
    summed = lax.psum_scatter(terms, "out", scatter_dimension=1, tiled=True)
    return summed + b_out.astype(jnp.float32)


def solution(mesh):
    placed = (
        P("tok", ("ka", "out")),
        P("tok"),
        P(("ka", "tok"), "out"),
        P(("out", "ka")),
        P(("out", "tok"), "ka"),
        P(("ka", "out")),
    )
    return jax.shard_map(
        shards, mesh=mesh, in_specs=placed, out_specs=P("tok", ("ka", "out")), check_vma=False
    )
```

profile of v0, /device:TPU:0, one launch (start us, length us, event | category | flops | bytes accessed | tf_op | source)
XLA Modules:
  0.0 1123.8 jit_solution(12351789201548837394)
XLA Ops:
  6.5 0.0 all-gather.5.cloned.1.call-start
  6.5 0.7 all-gather.5.cloned.1.call-update
  7.3 0.0 all-gather.7.cloned.1.call-start
  7.3 0.7 all-gather.7.cloned.1.call-update
  8.0 0.0 reduce-scatter.3.cloned.1.call-start
  8.1 13.4 %all-gather.5.cloned.1.call-done = bf16[256,3072]{1,0:T(8,128)(2,1)} async-done(((bf16[256,1536]{1,0:T(8,128)(2,1)}), bf16[256,3072]{1,0:T(8,128)(2,1)}) %all-gather.5.cloned.1.call-update) | async-done | bytes 1572880 | tf_op jit(solution)/shard_map/all_gather | solution.py:22
  21.4 650.2 %all-gather.7.cloned.1.call-done = bf16[3072,12288]{1,0:T(8,128)(2,1)} async-done(((bf16[768,12288]{1,0:T(8,128)(2,1)}), bf16[3072,12288]{1,0:T(8,128)(2,1)}) %all-gather.7.cloned.1.call-update) | async-done | bytes 75497488 | tf_op jit(solution)/shard_map/all_gather | solution.py:23
  671.6 31.1 %convolution_convert_fusion = bf16[256,12288]{1,0:T(8,128)(2,1)} fusion(bf16[256,3072]{1,0:T(8,128)(2,1)} %all-gather.5.cloned.1.call-done, bf16[3072,12288]{1,0:T(8,128)(2,1)} %all-gather.7.cloned.1.call-done), kind=kOutput, calls=%fused_computation.1 | convolution fusion | flops 19330498560 | bytes 83361792 | tf_op jit(solution)/shard_map/dot_general | solution.py:24
  702.7 0.0 reduce-scatter.3.cloned.1.call-update
  702.8 0.0 copy-start
  702.8 0.0 all-gather.11.cloned.1.call-start
  702.8 0.5 all-gather.11.cloned.1.call-update
  703.4 0.0 all-gather.9.cloned.1.call-start
  703.4 0.1 copy-done
  704.1 0.1 fusion.6
  704.2 109.4 %reduce-scatter.3.cloned.1.call-done = bf16[256,3072]{1,0:T(8,128)(2,1)} async-done(((bf16[256,12288]{1,0:T(8,128)(2,1)}), bf16[256,3072]{1,0:T(8,128)(2,1)}) %reduce-scatter.3.cloned.1.call-update) | async-done | bytes 1572880 | tf_op jit(solution)/shard_map/reduce_scatter | solution.py:25
  813.7 1.7 add_convert_fusion
  815.4 0.7 copy.11
  816.1 0.9 fusion.14
  817.0 2.0 convolution_convert_fusion.1
  819.0 0.0 all-gather.9.cloned.1.call-update
  819.0 0.0 reduce-scatter.5.cloned.1.call-start
  819.0 224.6 %all-gather.11.cloned.1.call-done = bf16[4096,3072]{1,0:T(8,128)(2,1)} async-done(((bf16[1024,3072]{1,0:T(8,128)(2,1)}), bf16[4096,3072]{1,0:T(8,128)(2,1)}) %all-gather.11.cloned.1.call-update) | async-done | bytes 25165840 | tf_op jit(solution)/shard_map/all_gather | solution.py:52
  1043.7 47.4 %all-gather.9.cloned.1.call-done = bf16[256,4096]{0,1:T(8,128)(2,1)} async-done(((bf16[256,1024]{0,1:T(8,128)(2,1)}), bf16[256,4096]{0,1:T(8,128)(2,1)}) %all-gather.9.cloned.1.call-update) | async-done | bytes 2097168 | tf_op jit(solution)/shard_map/all_gather | solution.py:49
  1091.1 13.3 %fusion.15 = f32[256,3072]{1,0:T(8,128)} fusion(bf16[256,4096]{0,1:T(8,128)(2,1)} %all-gather.9.cloned.1.call-done, bf16[4096,3072]{1,0:T(8,128)(2,1)} %all-gather.11.cloned.1.call-done), kind=kOutput, calls=%fused_computation.25 | convolution fusion | flops 6442450944 | bytes 30408704 | tf_op jit(solution)/shard_map/dot_general | solution.py:50
  1104.4 0.0 copy-start.1
  1104.4 0.0 reduce-scatter.5.cloned.1.call-update
  1104.4 0.7 copy-done.1
  1105.1 9.1 reduce-scatter.5.cloned.1.call-done
  1114.2 2.7 broadcast_add_fusion
  (3 shorter events, 0.0 us)
Async XLA Ops:
  6.5 14.9 %all-gather.5.cloned.1.call-start = ((), (), s32[]{:S(2)}) async-start(), calls=%async_computation.2 | async-start | bytes 2359296 | tf_op jit(solution)/shard_map/all_gather | solution.py:22
  7.3 664.4 %all-gather.7.cloned.1.call-start = ((), (), s32[]{:S(2)}) async-start(), calls=%async_computation.3 | async-start | bytes 94371840 | tf_op jit(solution)/shard_map/all_gather | solution.py:23
  8.0 805.7 %reduce-scatter.3.cloned.1.call-start = ((), (), s32[]{:S(2)}) async-start(), calls=%async_computation.4 | async-start | bytes 7864320 | tf_op jit(solution)/shard_map/reduce_scatter | solution.py:25
  702.8 0.7 copy-start
  702.8 340.9 %all-gather.11.cloned.1.call-start = ((), (), s32[]{:S(2)}) async-start(), calls=%async_computation.6 | async-start | bytes 31457280 | tf_op jit(solution)/shard_map/all_gather | solution.py:52
  703.4 387.7 %all-gather.9.cloned.1.call-start = ((), (), s32[]{:S(2)}) async-start(), calls=%async_computation.5 | async-start | bytes 2621440 | tf_op jit(solution)/shard_map/all_gather | solution.py:49
  819.0 295.2 %reduce-scatter.5.cloned.1.call-start = ((), (), s32[]{:S(2)}) async-start(), calls=%async_computation.7 | async-start | bytes 4718592 | tf_op jit(solution)/shard_map/reduce_scatter | solution.py:55
  1104.4 0.7 copy-start.1
Sparse Core Ops, SparseCore 0:
  8.9 12.4 all-gather.4
  23.3 648.2 all-gather.6
  702.9 110.7 reduce-scatter.2
  815.4 228.2 all-gather.10
  1045.1 45.9 all-gather.8
  1104.5 9.5 reduce-scatter.4
where the time goes:
time: 1120 us
  waiting for transfers between devices  1060 us (95%)
  matrix products  47.3 us (4%)
  between operations  14.2 us (1%)
    all_gather x1, waiting for transfers between devices, shards(): w_block = lax.all_gather(w_qkv, 'tok', axis=0, tiled=True)  650 us
    all_gather x1, waiting for transfers between devices, shards(): lax.all_gather(w_out, 'tok', axis=0, tiled=True)  225 us
    reduce_scatter x1, waiting for transfers between devices, shards(): lax.psum_scatter(partial_value.astype(jnp.bfloat16), 'ka', scatter_dimens...  109 us
    all_gather x1, waiting for transfers between devices, shards(): head_group = lax.all_gather(context, 'ka', axis=1, tiled=True)  47.4 us
    dot_general x1, matrix products, shards(): partial_value = jnp.dot(panel, w_block, preferred_element_type=jnp.float32)  31.1 us
  transfers between devices with their start and end apart: 6, of which 6 were waited for; matrix products, arithmetic and copies ran while one was open for 0% of the time, Pallas kernels for 0%

commit v1 on v0

--- a/solution.py
+++ b/solution.py
@@ -46,7 +46,12 @@
         "phst,pthd->pshd", prob_rows, table[:, :, :, 2], preferred_element_type=jnp.float32
     )
     context = context.astype(jnp.bfloat16).reshape(row_count, heads_dev * HD)
-    head_group = lax.all_gather(context, "ka", axis=1, tiled=True)
+    ring = [context]
+    for hop in range(3):
+        ring.append(lax.ppermute(ring[-1], "ka", [(dev, (dev + 1) % 4) for dev in range(4)]))
+    head_group = jnp.roll(
+        jnp.concatenate(ring[::-1], axis=1), (lax.axis_index("ka") + 1) * ring[0].shape[1], axis=1
+    )
     terms = jnp.dot(
         head_group,
         lax.all_gather(w_out, "tok", axis=0, tiled=True),

time: 1120 us -> 1080 us (0.964)
  waiting for transfers between devices: 1060 us -> 1000 us
    all_gather x1, waiting for transfers between devices: 225 us -> 175 us  [shards(): lax.all_gather(w_out, 'tok', axis=0, tiled=True)]
    all_gather x1 -> x0, waiting for transfers between devices: 47.4 us -> none  [shards(): head_group = lax.all_gather(context, 'ka', axis=1, tiled=True)]
    ppermute x0 -> x3, waiting for transfers between devices: none -> 42.4 us  [shards(): lax.ppermute(ring[-1], 'ka', [(dev, (dev + 1) % 4) for dev in range(4)])]
  transfers between devices with their start and end apart: 6 -> 8, of which waited for: 6 -> 8; matrix products, arithmetic and copies ran while one was open for 0% -> 1% of each run, Pallas kernels for 0% -> 0%
where the time goes in v1:
time: 1080 us
  waiting for transfers between devices  1000 us (93%)
  matrix products  46.5 us (4%)
  between operations  13.8 us (1%)
    all_gather x1, waiting for transfers between devices, shards(): w_block = lax.all_gather(w_qkv, 'tok', axis=0, tiled=True)  650 us
    all_gather x1, waiting for transfers between devices, shards(): lax.all_gather(w_out, 'tok', axis=0, tiled=True)  175 us
    reduce_scatter x1, waiting for transfers between devices, shards(): lax.psum_scatter(partial_value.astype(jnp.bfloat16), 'ka', scatter_dimens...  109 us
    ppermute x3, waiting for transfers between devices, shards(): lax.ppermute(ring[-1], 'ka', [(dev, (dev + 1) % 4) for dev in range(4)])  42.4 us
    dot_general x1, matrix products, shards(): partial_value = jnp.dot(panel, w_block, preferred_element_type=jnp.float32)  31.1 us
  transfers between devices with their start and end apart: 8, of which 8 were waited for; matrix products, arithmetic and copies ran while one was open for 1% of the time, Pallas kernels for 0%

profile of v1, /device:TPU:0, one launch (start us, length us, event | category | flops | bytes accessed | tf_op | source)
XLA Modules:
  0.0 1077.4 jit_solution(6226893992701199469)
XLA Ops:
  6.5 0.7 all-gather.4.cloned.1.call-update
  7.3 0.7 all-gather.6.cloned.1.call-update
  8.0 0.0 reduce-scatter.3.cloned.1.call-start
  8.1 13.4 %all-gather.4.cloned.1.call-done = bf16[256,3072]{1,0:T(8,128)(2,1)} async-done(((bf16[256,1536]{1,0:T(8,128)(2,1)}), bf16[256,3072]{1,0:T(8,128)(2,1)}) %all-gather.4.cloned.1.call-update) | async-done | bytes 1572880 | tf_op jit(solution)/shard_map/all_gather | solution.py:22
  21.4 650.2 %all-gather.6.cloned.1.call-done = bf16[3072,12288]{1,0:T(8,128)(2,1)} async-done(((bf16[768,12288]{1,0:T(8,128)(2,1)}), bf16[3072,12288]{1,0:T(8,128)(2,1)}) %all-gather.6.cloned.1.call-update) | async-done | bytes 75497488 | tf_op jit(solution)/shard_map/all_gather | solution.py:23
  671.6 31.1 %convolution_convert_fusion = bf16[256,12288]{1,0:T(8,128)(2,1)} fusion(bf16[256,3072]{1,0:T(8,128)(2,1)} %all-gather.4.cloned.1.call-done, bf16[3072,12288]{1,0:T(8,128)(2,1)} %all-gather.6.cloned.1.call-done), kind=kOutput, calls=%fused_computation.1 | convolution fusion | flops 19330498560 | bytes 83361792 | tf_op jit(solution)/shard_map/dot_general | solution.py:24
  702.8 0.0 all-gather.8.cloned.1.call-start
  702.8 0.5 all-gather.8.cloned.1.call-update
  703.4 0.1 copy-done
  704.1 0.1 fusion.8
  704.2 109.4 %reduce-scatter.3.cloned.1.call-done = bf16[256,3072]{1,0:T(8,128)(2,1)} async-done(((bf16[256,12288]{1,0:T(8,128)(2,1)}), bf16[256,3072]{1,0:T(8,128)(2,1)}) %reduce-scatter.3.cloned.1.call-update) | async-done | bytes 1572880 | tf_op jit(solution)/shard_map/reduce_scatter | solution.py:25
  813.7 1.7 add_convert_fusion
  815.4 0.7 copy.11
  816.1 0.9 fusion.17
  817.0 1.2 convolution_convert_fusion.1
  818.2 1.5 collective-permute-start
  819.7 14.0 %collective-permute-done = bf16[256,1024]{0,1:T(8,128)(2,1)S(1)} collective-permute-done((bf16[256,1024]{0,1:T(8,128)(2,1)S(1)}, bf16[256,1024]{0,1:T(8,128)(2,1)S(1)}, u32[]{:S(2)}, u32[]{:S(2)}) %collective-permute-start) | collective-permute-done | bytes 524320 | tf_op jit(solution)/shard_map/ppermute | solution.py:51
  833.7 14.6 %collective-permute-done.1 = bf16[256,1024]{0,1:T(8,128)(2,1)S(1)} collective-permute-done((bf16[256,1024]{0,1:T(8,128)(2,1)S(1)}, bf16[256,1024]{0,1:T(8,128)(2,1)S(1)}, u32[]{:S(2)}, u32[]{:S(2)}) %collective-permute-start.1) | collective-permute-done | bytes 524320 | tf_op jit(solution)/shard_map/ppermute | solution.py:51
  848.4 13.7 %collective-permute-done.2 = bf16[256,1024]{0,1:T(8,128)(2,1)S(1)} collective-permute-done((bf16[256,1024]{0,1:T(8,128)(2,1)S(1)}, bf16[256,1024]{0,1:T(8,128)(2,1)S(1)}, u32[]{:S(2)}, u32[]{:S(2)}) %collective-permute-start.2) | collective-permute-done | bytes 524320 | tf_op jit(solution)/shard_map/ppermute | solution.py:51
  862.1 0.9 constant_dynamic-update-slice_fusion.7
  863.0 0.9 constant_dynamic-update-slice_fusion.6
  863.9 0.8 constant_dynamic-update-slice_fusion.5
  864.7 0.8 constant_dynamic-update-slice_fusion.4
  865.5 0.9 constant_dynamic-update-slice_fusion.3
  866.3 0.8 constant_dynamic-update-slice_fusion.2
  867.2 0.8 constant_dynamic-update-slice_fusion.1
  868.0 0.8 constant_dynamic-update-slice_fusion
  868.8 174.9 %all-gather.8.cloned.1.call-done = bf16[4096,3072]{1,0:T(8,128)(2,1)} async-done(((bf16[1024,3072]{1,0:T(8,128)(2,1)}), bf16[4096,3072]{1,0:T(8,128)(2,1)}) %all-gather.8.cloned.1.call-update) | async-done | bytes 25165840 | tf_op jit(solution)/shard_map/all_gather | solution.py:57
  1043.7 13.3 %fusion.1 = f32[256,3072]{1,0:T(8,128)} fusion(bf16[4096,3072]{1,0:T(8,128)(2,1)} %all-gather.8.cloned.1.call-done, bf16[256,8192]{0,1:T(8,128)(2,1)} %constant_dynamic-update-slice_fusion, s32[]{:T(128)S(6)} %select_n.20), kind=kOutput, calls=%fused_computation.3 | convolution fusion | flops 6442450944 | bytes 30408708 | tf_op jit(solution)/shard_map/dot_general | solution.py:55
  1057.0 0.7 copy-done.1
  1057.7 10.4 reduce-scatter.5.cloned.1.call-done
  1068.1 2.7 broadcast_add_fusion
  (12 shorter events, 0.1 us)
Async XLA Ops:
  6.5 14.9 %all-gather.4.cloned.1.call-start = ((), (), s32[]{:S(2)}) async-start(), calls=%async_computation.2 | async-start | bytes 2359296 | tf_op jit(solution)/shard_map/all_gather | solution.py:22
  7.3 664.4 %all-gather.6.cloned.1.call-start = ((), (), s32[]{:S(2)}) async-start(), calls=%async_computation.3 | async-start | bytes 94371840 | tf_op jit(solution)/shard_map/all_gather | solution.py:23
  8.0 805.7 %reduce-scatter.3.cloned.1.call-start = ((), (), s32[]{:S(2)}) async-start(), calls=%async_computation.4 | async-start | bytes 7864320 | tf_op jit(solution)/shard_map/reduce_scatter | solution.py:25
  702.8 0.7 copy-start
  702.8 340.9 %all-gather.8.cloned.1.call-start = ((), (), s32[]{:S(2)}) async-start(), calls=%async_computation.5 | async-start | bytes 31457280 | tf_op jit(solution)/shard_map/all_gather | solution.py:57
  703.4 364.7 %reduce-scatter.5.cloned.1.call-start = ((), (), s32[]{:S(2)}) async-start(), calls=%async_computation.6 | async-start | bytes 4718592 | tf_op jit(solution)/shard_map/reduce_scatter | solution.py:60
  818.2 15.6 %collective-permute-start = (bf16[256,1024]{0,1:T(8,128)(2,1)S(1)}, bf16[256,1024]{0,1:T(8,128)(2,1)S(1)}, u32[]{:S(2)}, u32[]{:S(2)}) collective-permute-start(bf16[256,1024]{0,1:T(8,128)(2,1)S(1)} %bitcast.48), channel_id=1, source_target_pairs={{0,2},{2,4},{4,6},{6,0},{1,3},{3,5},{5,7},{7,1},{8,10},{10,12},{12... | collective-permute-start | bytes 1572872 | tf_op jit(solution)/shard_map/ppermute | solution.py:51
  833.7 14.7 %collective-permute-start.1 = (bf16[256,1024]{0,1:T(8,128)(2,1)S(1)}, bf16[256,1024]{0,1:T(8,128)(2,1)S(1)}, u32[]{:S(2)}, u32[]{:S(2)}) collective-permute-start(bf16[256,1024]{0,1:T(8,128)(2,1)S(1)} %collective-permute-done), channel_id=1, source_target_pairs={{0,2},{2,4},{4,6},{6,0},{1,3},{3,5},{5,7},{7,1},{8,10},{10,12},{12... | collective-permute-start | bytes 1572872 | tf_op jit(solution)/shard_map/ppermute | solution.py:51
  848.4 13.7 %collective-permute-start.2 = (bf16[256,1024]{0,1:T(8,128)(2,1)S(1)}, bf16[256,1024]{0,1:T(8,128)(2,1)S(1)}, u32[]{:S(2)}, u32[]{:S(2)}) collective-permute-start(bf16[256,1024]{0,1:T(8,128)(2,1)S(1)} %collective-permute-done.1), channel_id=1, source_target_pairs={{0,2},{2,4},{4,6},{6,0},{1,3},{3,5},{5,7},{7,1},{8,10},{10,12},{12... | collective-permute-start | bytes 1572872 | tf_op jit(solution)/shard_map/ppermute | solution.py:51
  1057.0 0.7 copy-start.1
Sparse Core Ops, SparseCore 0:
  8.9 12.4 all-gather.3
  23.3 648.2 all-gather.5
  702.9 110.7 reduce-scatter.2
  815.4 228.2 all-gather.7
  1057.1 10.8 reduce-scatter.4
